TPU v7x, 32 devices: a whole 2x2x4 slice. The times are simulated.
32 devices in a mesh: row: 4 (over x, core), col: 8 (over z, y).
Axes of the slice: x: 2, y: 2, z: 4, core: 2. Of those that a mesh axis runs over, the one named last changes fastest.
Arguments:
- right_side: float32 [64, 16384], P(None, 'row'), may hold values from -8 to 8
- blocks: bfloat16 [3072, 128, 128], P(('row', 'col')), may hold values from -1 to 1
- targets: int32 [3072, 1], P(('row', 'col')), may hold values from 0 to 7; in each aligned block of 96 rows (0 to 95, 96 to 191, ...) at most 24 rows name the same one
- tile_rows: int32 [3072], P(('row', 'col')), may hold values from 0 to 31
- tile_cols: int32 [3072], P(('row', 'col')), may hold values from 0 to 31
Outputs:
- solution: float32 [64, 8, 4096], P(None, 'col', 'row')
- phibar: float32 [64], replicated
Inputs may be any that keep to these rules, and one draw needn't show every extreme that they name: `targets`: among the 96 blocks of one device, at most 24 name the same grid column, and some grid column is named exactly 24 times by some device.
All inputs are finite; a program needn't handle non-finite values.
Results may differ from a plain program's by a relative error of at most 0.0032.
Values may be sent and summed in bfloat16 or wider, within the bound.
No kernel may reach another device: no remote copies, remote signals or barrier semaphores. Data moves between devices by JAX's collectives and lax.ppermute only.
A program may use at most 128 MiB of HBM per device.

v0:
```python
import jax
import jax.numpy as jnp
from jax import lax
from jax.sharding import PartitionSpec as P

TC = 32
ITERS = 4
EPSILON = 1e-06


def gather_tiles(vector_bf, indices, block_size):
    snapshots, extent = vector_bf.shape
    vector_tiles = vector_bf.reshape(snapshots, extent // block_size, block_size)
    return jnp.take(vector_tiles, indices, axis=1)


def place_terms(weighted, indices, n_out):
    snapshots, number, block_size = weighted.shape
    onehot = (indices[:, None] == jnp.arange(n_out, dtype=jnp.int32)[None, :]).astype(jnp.float32)
    summed = jnp.einsum("ksi,st->kti", weighted, onehot, precision=lax.Precision.HIGHEST)
    return summed.reshape(snapshots, n_out * block_size)


def forward_terms(vector_bf, blocks, row_index, col_index, n_out):
    picked = gather_tiles(vector_bf, col_index, blocks.shape[1])
    weighted = jnp.einsum("sij,ksj->ksi", blocks, picked, preferred_element_type=jnp.float32)
    return place_terms(weighted, row_index, n_out)


def backward_terms(vector_bf, blocks, row_index, col_index, n_out):
    picked = gather_tiles(vector_bf, row_index, blocks.shape[1])
    weighted = jnp.einsum("sji,ksj->ksi", blocks, picked, preferred_element_type=jnp.float32)
    return place_terms(weighted, col_index, n_out)


def per_device(right_side, blocks, targets, tile_rows, tile_cols):
    col_count = lax.axis_size("col")
    row_count = lax.axis_size("row")
    block_size = blocks.shape[1]
    snapshots = right_side.shape[0]
    row_tiles = right_side.shape[1] // block_size
    own_count = blocks.shape[0]
    capacity = 2 * own_count // col_count
    target = targets[:, 0]
    matches = (target[:, None] == jnp.arange(col_count, dtype=jnp.int32)[None, :]).astype(jnp.int32)
    before = jnp.cumsum(matches, axis=0) - matches
    slot_index = target * capacity + jnp.sum(before * matches, axis=1)
    outgoing = (
        jnp.zeros((col_count * capacity, block_size, block_size), blocks.dtype)
        .at[slot_index]
        .set(blocks)
    )
    places = (
        jnp.zeros((col_count * capacity, 2), jnp.int32)
        .at[slot_index]
        .set(jnp.stack([tile_rows, tile_cols], axis=1))
    )
    arrived, arrived_places = (
        lax.all_to_all(
            outgoing.reshape(col_count, capacity, block_size, block_size),
            "col",
            split_axis=0,
            concat_axis=0,
            tiled=True,
        ),
        lax.all_to_all(
            places.reshape(col_count, capacity, 2), "col", split_axis=0, concat_axis=0, tiled=True
        ),
    )
    work_blocks = arrived.reshape(col_count * capacity, block_size, block_size)
    flat_places = arrived_places.reshape(col_count * capacity, 2)
    work_rows = flat_places[:, 0]
    work_cols = flat_places[:, 1]

    def backward(left_bf):
        return backward_terms(left_bf, work_blocks, work_rows, work_cols, TC)

    def sum_right(partial_value):
        return lax.psum(partial_value, "row")

    def finish_left(unscaled, need_form):
        squares = jnp.sum(unscaled * unscaled, axis=1)
        total = lax.psum(squares, "row")
        beta_norm = jnp.sqrt(total + EPSILON)
        scaled = unscaled / beta_norm[:, None]
        rounded = None
        if need_form:
            rounded = scaled.astype(jnp.bfloat16)
        return (beta_norm, scaled, rounded)

    def finish_right(unscaled):
        squares = jnp.sum(unscaled * unscaled, axis=1)
        total = lax.psum(squares, "col")
        alpha_norm = jnp.sqrt(total + EPSILON)
        scaled = unscaled / alpha_norm[:, None]
        rounded = scaled.astype(jnp.bfloat16)
        return (alpha_norm, scaled, rounded)

    beta_norm, left_vec, left_bf = finish_left(right_side, True)
    alpha_norm, right_vec, right_bf = finish_right(sum_right(backward(left_bf)))
    search = right_vec
    solution = jnp.zeros_like(right_vec)
    phibar = beta_norm
    rhobar = alpha_norm
    for iteration in range(ITERS):
        last_turn = iteration + 1 == ITERS
        unscaled = (
            lax.psum(forward_terms(right_bf, work_blocks, work_rows, work_cols, row_tiles), "col")
            - alpha_norm[:, None] * left_vec
        )
        beta_norm, left_vec, left_bf = finish_left(unscaled, not last_turn)
        rho_value = jnp.sqrt(rhobar * rhobar + beta_norm * beta_norm)
        cosine = rhobar / rho_value
        sine_value = beta_norm / rho_value
        phi_value = cosine * phibar
        phibar = sine_value * phibar
        solution = solution + (phi_value / rho_value)[:, None] * search
        if not last_turn:
            unscaled = sum_right(backward(left_bf)) - beta_norm[:, None] * right_vec
            alpha_norm, right_vec, right_bf = finish_right(unscaled)
            theta_value = sine_value * alpha_norm
            rhobar = -cosine * alpha_norm
            search = right_vec - (theta_value / rho_value)[:, None] * search
    share_len = solution.shape[1] // row_count
    solution = lax.dynamic_slice_in_dim(solution, lax.axis_index("row") * share_len, share_len, 1)
    return (solution.reshape(snapshots, 1, solution.shape[1]), phibar)


def solution(mesh):
    placed = (
        P(None, "row"),
        P(("row", "col"), None, None),
        P(("row", "col"), None),
        P(("row", "col")),
        P(("row", "col")),
    )
    return jax.shard_map(
        per_device,
        mesh=mesh,
        in_specs=placed,
        out_specs=(P(None, "col", "row"), P()),
        check_vma=False,
    )
```

profile of v0, /device:TPU:0, one launch (start us, length us, event | category | flops | bytes accessed | tf_op | source)
XLA Modules:
  0.0 906.9 jit_solution(17280355181446882380)
XLA Ops:
  11.9 7.3 all-to-all-start
  19.2 4.2 broadcast_in_dim.14
  23.4 14.7 %scatter_fusion = bf16[192,128,128]{2,1,0:T(8,128)(2,1)} fusion(bf16[192,128,128]{2,1,0:T(8,128)(2,1)} %broadcast_in_dim.14, s32[96]{0:T(128)S(1)} %fusion.105, bf16[96,128,128]{2,1,0:T(8,128)(2,1)} %param.8), kind=kCustom, calls=%fused_computation.9 | custom fusion | bytes 9437568 | tf_op jit(solution)/shard_map/scatter | solution.py:51
  38.1 6.1 all-to-all-start.1
  44.4 5.7 psum.119
  50.5 2.7 gather_fusion
  53.3 128.6 %all-to-all-done.1 = bf16[8,24,128,128]{3,2,1,0:T(8,128)(2,1)} async-done(((bf16[8,24,128,128]{3,2,1,0:T(8,128)(2,1)}), bf16[8,24,128,128]{3,2,1,0:T(8,128)(2,1)}, u32[]{:S(2)}, u32[]{:S(2)}) %all-to-all-start.1) | async-done | bytes 6291488 | tf_op jit(solution)/shard_map/all_to_all | solution.py:59
  181.9 5.6 fusion.48
  187.5 5.7 fusion.14
  193.2 1.6 copy.119
  194.9 35.2 %all-reduce.9.cloned.1.call-done = f32[64,4096]{1,0:T(8,128)} async-done(((f32[64,4096]{1,0:T(8,128)}), f32[64,4096]{1,0:T(8,128)}) %all-reduce.9.cloned.1.call-update) | async-done | bytes 1048592 | tf_op jit(solution)/shard_map/psum | solution.py:79
  231.5 21.5 %psum.121 = f32[64]{0:T(128)S(1)} all-reduce(f32[64]{0:T(128)S(1)} %multiply_reduce_fusion.7), channel_id=1, replica_groups=mesh['row'=4,'col'=8] {'col'}, use_global_device_ids=true, to_apply=%region_8.10 | all-reduce | flops 64 | bytes 512 | tf_op jit(solution)/shard_map/psum | solution.py:93
  254.6 2.8 gather_fusion.1
  257.4 8.1 fusion.51
  265.4 5.7 fusion.12
  271.2 1.6 copy.118
  272.8 75.0 %all-reduce.11.cloned.1.call-done = f32[64,4096]{1,0:T(8,128)} async-done(((f32[64,4096]{1,0:T(8,128)}), f32[64,4096]{1,0:T(8,128)}) %all-reduce.11.cloned.1.call-update) | async-done | bytes 1048592 | tf_op jit(solution)/shard_map/psum | solution.py:108
  347.9 2.5 multiply_reduce_fusion.6
  350.4 6.1 psum.123
  357.9 2.8 gather_fusion.2
  360.7 5.6 fusion.54
  366.3 5.7 fusion.10
  372.0 1.6 copy.117
  373.7 35.8 %all-reduce.13.cloned.1.call-done = f32[64,4096]{1,0:T(8,128)} async-done(((f32[64,4096]{1,0:T(8,128)}), f32[64,4096]{1,0:T(8,128)}) %all-reduce.13.cloned.1.call-update) | async-done | bytes 1048592 | tf_op jit(solution)/shard_map/psum | solution.py:79
  409.5 1.5 multiply_reduce_fusion.5
  411.0 21.8 %psum.125 = f32[64]{0:T(128)S(1)} all-reduce(f32[64]{0:T(128)S(1)} %multiply_reduce_fusion.5), channel_id=1, replica_groups=mesh['row'=4,'col'=8] {'col'}, use_global_device_ids=true, to_apply=%region_14.16 | all-reduce | flops 64 | bytes 512 | tf_op jit(solution)/shard_map/psum | solution.py:93
  432.8 1.5 convert_bitcast_fusion.4
  434.5 2.8 gather_fusion.3
  437.2 8.1 fusion.57
  445.3 5.8 fusion.8
  451.1 1.6 copy.116
  452.8 75.0 %all-reduce.15.cloned.1.call-done = f32[64,4096]{1,0:T(8,128)} async-done(((f32[64,4096]{1,0:T(8,128)}), f32[64,4096]{1,0:T(8,128)}) %all-reduce.15.cloned.1.call-update) | async-done | bytes 1048592 | tf_op jit(solution)/shard_map/psum | solution.py:108
  527.8 2.6 multiply_reduce_fusion.4
  530.3 6.1 psum.127
  537.8 2.8 gather_fusion.4
  540.6 5.6 fusion.60
  546.1 5.8 fusion.6
  551.9 1.6 copy.115
  553.6 35.8 %all-reduce.17.cloned.1.call-done = f32[64,4096]{1,0:T(8,128)} async-done(((f32[64,4096]{1,0:T(8,128)}), f32[64,4096]{1,0:T(8,128)}) %all-reduce.17.cloned.1.call-update) | async-done | bytes 1048592 | tf_op jit(solution)/shard_map/psum | solution.py:79
  589.4 1.5 multiply_reduce_fusion.3
  591.0 21.6 %psum.129 = f32[64]{0:T(128)S(1)} all-reduce(f32[64]{0:T(128)S(1)} %multiply_reduce_fusion.3), channel_id=1, replica_groups=mesh['row'=4,'col'=8] {'col'}, use_global_device_ids=true, to_apply=%region_20.22 | all-reduce | flops 64 | bytes 512 | tf_op jit(solution)/shard_map/psum | solution.py:93
  612.5 2.5 convert_bitcast_fusion.2
  615.1 2.8 gather_fusion.5
  617.9 8.1 fusion.63
  626.0 5.8 fusion.4
  631.8 1.6 copy.114
  633.5 75.0 %all-reduce.19.cloned.1.call-done = f32[64,4096]{1,0:T(8,128)} async-done(((f32[64,4096]{1,0:T(8,128)}), f32[64,4096]{1,0:T(8,128)}) %all-reduce.19.cloned.1.call-update) | async-done | bytes 1048592 | tf_op jit(solution)/shard_map/psum | solution.py:108
  708.5 2.6 multiply_reduce_fusion.2
  711.0 6.3 psum.131
  718.7 2.8 gather_fusion.6
  721.5 5.6 fusion.66
  727.1 5.8 fusion.2
  732.9 1.6 copy.113
  734.5 35.8 %all-reduce.21.cloned.1.call-done = f32[64,4096]{1,0:T(8,128)} async-done(((f32[64,4096]{1,0:T(8,128)}), f32[64,4096]{1,0:T(8,128)}) %all-reduce.21.cloned.1.call-update) | async-done | bytes 1048592 | tf_op jit(solution)/shard_map/psum | solution.py:79
  770.4 1.5 multiply_reduce_fusion.1
  771.9 21.5 %psum.133 = f32[64]{0:T(128)S(1)} all-reduce(f32[64]{0:T(128)S(1)} %multiply_reduce_fusion.1), channel_id=1, replica_groups=mesh['row'=4,'col'=8] {'col'}, use_global_device_ids=true, to_apply=%region_26.28 | all-reduce | flops 64 | bytes 512 | tf_op jit(solution)/shard_map/psum | solution.py:93
  793.4 2.5 convert_bitcast_fusion
  796.0 2.8 gather_fusion.7
  798.8 8.1 fusion.69
  806.9 5.8 fusion
  812.7 1.6 copy.112
  814.4 75.1 %all-reduce.23.cloned.1.call-done = f32[64,4096]{1,0:T(8,128)} async-done(((f32[64,4096]{1,0:T(8,128)}), f32[64,4096]{1,0:T(8,128)}) %all-reduce.23.cloned.1.call-update) | async-done | bytes 1048592 | tf_op jit(solution)/shard_map/psum | solution.py:108
  889.4 1.6 multiply_reduce_fusion
  891.0 5.9 psum.135
  (68 shorter events, 16.4 us)
Async XLA Ops:
  11.9 26.2 %all-to-all-start = ((s32[8,24,2]{1,2,0:T(2,128)}), s32[8,24,2]{1,2,0:T(2,128)S(1)}, u32[]{:S(2)}, u32[]{:S(2)}) async-start(s32[8,24,2]{1,2,0:T(2,128)} %copy.46), calls=%async_computation | async-start | bytes 16384 | tf_op jit(solution)/shard_map/all_to_all | solution.py:66
  38.1 6.1 copy-start.1
  38.1 143.8 %all-to-all-start.1 = ((bf16[8,24,128,128]{3,2,1,0:T(8,128)(2,1)}), bf16[8,24,128,128]{3,2,1,0:T(8,128)(2,1)}, u32[]{:S(2)}, u32[]{:S(2)}) async-start(bf16[8,24,128,128]{3,2,1,0:T(8,128)(2,1)} %bitcast.172), calls=%async_computation.1 | async-start | bytes 12582912 | tf_op jit(solution)/shard_map/all_to_all | solution.py:59
  44.2 185.9 %all-reduce.9.cloned.1.call-start = ((), (), s32[]{:S(2)}) async-start(), calls=%async_computation.2 | async-start | bytes 2097152 | tf_op jit(solution)/shard_map/psum | solution.py:79
  194.8 153.0 %all-reduce.11.cloned.1.call-start = ((), (), s32[]{:S(2)}) async-start(), calls=%async_computation.3 | async-start | bytes 2097152 | tf_op jit(solution)/shard_map/psum | solution.py:108
  272.8 136.7 %all-reduce.13.cloned.1.call-start = ((), (), s32[]{:S(2)}) async-start(), calls=%async_computation.4 | async-start | bytes 2097152 | tf_op jit(solution)/shard_map/psum | solution.py:79
  373.6 154.1 %all-reduce.15.cloned.1.call-start = ((), (), s32[]{:S(2)}) async-start(), calls=%async_computation.5 | async-start | bytes 2097152 | tf_op jit(solution)/shard_map/psum | solution.py:108
  451.1 76.6 %copy-start.4 = (f32[64,4096]{1,0:T(8,128)S(1)}, f32[64,4096]{1,0:T(8,128)}, u32[]{:S(2)}) copy-start(f32[64,4096]{1,0:T(8,128)} %get-tuple-element.25) | copy-start | bytes 3145732
  452.7 136.7 %all-reduce.17.cloned.1.call-start = ((), (), s32[]{:S(2)}) async-start(), calls=%async_computation.6 | async-start | bytes 2097152 | tf_op jit(solution)/shard_map/psum | solution.py:79
  553.5 154.9 %all-reduce.19.cloned.1.call-start = ((), (), s32[]{:S(2)}) async-start(), calls=%async_computation.7 | async-start | bytes 2097152 | tf_op jit(solution)/shard_map/psum | solution.py:108
  631.8 76.6 %copy-start.3 = (f32[64,4096]{1,0:T(8,128)S(1)}, f32[64,4096]{1,0:T(8,128)}, u32[]{:S(2)}) copy-start(f32[64,4096]{1,0:T(8,128)} %get-tuple-element.21) | copy-start | bytes 3145732
  633.4 136.9 %all-reduce.21.cloned.1.call-start = ((), (), s32[]{:S(2)}) async-start(), calls=%async_computation.8 | async-start | bytes 2097152 | tf_op jit(solution)/shard_map/psum | solution.py:79
  732.9 37.5 %copy-start = (f32[64,4096]{1,0:T(8,128)S(1)}, f32[64,4096]{1,0:T(8,128)}, u32[]{:S(2)}) copy-start(f32[64,4096]{1,0:T(8,128)} %get-tuple-element.19) | copy-start | bytes 3145732
  734.5 155.0 %all-reduce.23.cloned.1.call-start = ((), (), s32[]{:S(2)}) async-start(), calls=%async_computation.9 | async-start | bytes 2097152 | tf_op jit(solution)/shard_map/psum | solution.py:108
  812.7 76.8 %copy-start.2 = (f32[64,4096]{1,0:T(8,128)S(1)}, f32[64,4096]{1,0:T(8,128)}, u32[]{:S(2)}) copy-start(f32[64,4096]{1,0:T(8,128)} %get-tuple-element.17) | copy-start | bytes 3145732
Sparse Core Ops, SparseCore 0:
  194.9 35.0 all-reduce.8
  272.9 74.8 all-reduce.10
  373.7 35.7 all-reduce.12
  452.9 74.8 all-reduce.14
  553.7 35.7 all-reduce.16
  633.5 74.8 all-reduce.18
  734.6 35.7 all-reduce.20
  814.5 74.9 all-reduce.22
where the time goes:
time: 916 us; the launch traced here: 907 us
  waiting for transfers between devices  571 us (62%)
  blocking collectives  116 us (13%)
  matrix products  101 us (11%)
  local copies, waits for them, and re-layouts  56.9 us (6%)
  other arithmetic  32.9 us (4%)
  between operations  14.7 us (2%)
  starting transfers between devices  13.7 us (1%)
    psum x4, waiting for transfers between devices, per_device(): lax.psum(forward_terms(right_bf, work_blocks, work_rows, work_cols, row_t...  300 us
    psum x4, waiting for transfers between devices, sum_right(): return lax.psum(partial_value, 'row')  143 us
    all_to_all x1, waiting for transfers between devices, per_device(): lax.all_to_all(outgoing.reshape(col_count, capacity, block_size, block_si...  129 us
    psum x4, blocking collectives, finish_right(): total = lax.psum(squares, 'col')  86.4 us
    dot_general x8, matrix products, place_terms(): jnp.einsum('ksi,st->kti', weighted, onehot, precision=lax.Precision.HIGHEST)  46.2 us
    dot_general x4, matrix products, forward_terms(): jnp.einsum('sij,ksj->ksi', blocks, picked, preferred_element_type=jnp.flo...  32.3 us
    psum x5, blocking collectives, finish_left(): total = lax.psum(squares, 'row')  30.1 us
    dot_general x4, matrix products, backward_terms(): jnp.einsum('sji,ksj->ksi', blocks, picked, preferred_element_type=jnp.flo...  22.3 us
  transfers between devices with their start and end apart: 10, of which 9 were waited for; matrix products, arithmetic and copies ran while one was open for 2% of the time, Pallas kernels for 0%

commit v1 on v0

--- a/solution.py
+++ b/solution.py
@@ -6,6 +6,19 @@
 TC = 32
 ITERS = 4
 EPSILON = 1e-06
+
+
+def render_chunk(work_x, k_dim, x_in):
+    mid_arr, z2 = (work_x.shape[:k_dim], work_x.shape[k_dim + 1 :])
+    return jnp.moveaxis(work_x.reshape(*mid_arr, x_in, -1, *z2), k_dim, 0)
+
+
+def supply_wall(point, on_dim):
+    point = jnp.moveaxis(point, 0, on_dim)
+    work_now = point.shape
+    return point.reshape(
+        *work_now[:on_dim], work_now[on_dim] * work_now[on_dim + 1], *work_now[on_dim + 2 :]
+    )
 
 
 def gather_tiles(vector_bf, indices, block_size):
@@ -55,14 +68,19 @@
         .at[slot_index]
         .set(jnp.stack([tile_rows, tile_cols], axis=1))
     )
+
+    def _obtain_counts(local_array, mesh_name, inputs, my_data):
+        tmp, local_now = (lax.axis_size(mesh_name), lax.axis_index(mesh_name))
+        taken_in = render_chunk(local_array, inputs, tmp)
+        found = [taken_in[local_now]]
+        for nth in range(1, tmp):
+            r1 = taken_in[(local_now + nth) % tmp]
+            found.append(lax.ppermute(r1, mesh_name, [(u, (u + nth) % tmp) for u in range(tmp)]))
+        taken_in = jnp.stack(found, axis=0)[(local_now - jnp.arange(tmp)) % tmp]
+        return supply_wall(taken_in, my_data)
+
     arrived, arrived_places = (
-        lax.all_to_all(
-            outgoing.reshape(col_count, capacity, block_size, block_size),
-            "col",
-            split_axis=0,
-            concat_axis=0,
-            tiled=True,
-        ),
+        _obtain_counts(outgoing.reshape(col_count, capacity, block_size, block_size), "col", 0, 0),
         lax.all_to_all(
             places.reshape(col_count, capacity, 2), "col", split_axis=0, concat_axis=0, tiled=True
         ),

time: 916 us -> 933 us (1.019)
  local copies, waits for them, and re-layouts: 56.9 us -> 81 us
    all_to_all x1 -> x0, waiting for transfers between devices: 129 us -> none  [per_device(): lax.all_to_all(outgoing.reshape(col_count, capacity, block_size, block_si...]
    all_to_all x1, waiting for transfers between devices: 0.01 us -> 103 us  [per_device(): lax.all_to_all(places.reshape(col_count, capacity, 2), 'col', split_axis=...]
    ppermute x0 -> x7, waiting for transfers between devices: none -> 19.8 us  [_obtain_counts(): lax.ppermute(r1, mesh_name, [(u, (u + nth) % tmp) for u in range(tmp)])]
    ppermute x0 -> x7, starting transfers between devices: none -> 13.5 us  [_obtain_counts(): lax.ppermute(r1, mesh_name, [(u, (u + nth) % tmp) for u in range(tmp)])]
    unnamed x18 -> x36, local copies, waits for them, and re-layouts: 12.7 us -> 24.6 us
  transfers between devices with their start and end apart: 10 -> 16, of which waited for: 9 -> 11; matrix products, arithmetic and copies ran while one was open for 2% -> 2% of each run, Pallas kernels for 0% -> 0%
where the time goes in v1:
time: 933 us; the launch traced here: 927 us
  waiting for transfers between devices  568 us (61%)
  blocking collectives  117 us (13%)
  matrix products  99.2 us (11%)
  local copies, waits for them, and re-layouts  81 us (9%)
  other arithmetic  30.4 us (3%)
  starting transfers between devices  17.2 us (2%)
  between operations  14.8 us (2%)
    psum x4, waiting for transfers between devices, per_device(): lax.psum(forward_terms(right_bf, work_blocks, work_rows, work_cols, row_t...  300 us
    psum x4, waiting for transfers between devices, sum_right(): return lax.psum(partial_value, 'row')  146 us
    all_to_all x1, waiting for transfers between devices, per_device(): lax.all_to_all(places.reshape(col_count, capacity, 2), 'col', split_axis=...  103 us
    psum x4, blocking collectives, finish_right(): total = lax.psum(squares, 'col')  86.4 us
    dot_general x8, matrix products, place_terms(): jnp.einsum('ksi,st->kti', weighted, onehot, precision=lax.Precision.HIGHEST)  46.4 us
    dot_general x4, matrix products, forward_terms(): jnp.einsum('sij,ksj->ksi', blocks, picked, preferred_element_type=jnp.flo...  32.3 us
    psum x5, blocking collectives, finish_left(): total = lax.psum(squares, 'row')  30.4 us
    unnamed x36, local copies, waits for them, and re-layouts  24.6 us
  transfers between devices with their start and end apart: 16, of which 11 were waited for; matrix products, arithmetic and copies ran while one was open for 2% of the time, Pallas kernels for 0%

profile of v1, /device:TPU:0, one launch (start us, length us, event | category | flops | bytes accessed | tf_op | source)
XLA Modules:
  0.0 927.4 jit_solution(14666452442117234669)
XLA Ops:
  9.8 4.2 broadcast_in_dim.14
  14.0 12.7 %scatter_fusion = bf16[192,128,128]{2,1,0:T(8,128)(2,1)} fusion(bf16[192,128,128]{2,1,0:T(8,128)(2,1)} %broadcast_in_dim.14, s32[96]{0:T(128)S(1)} %fusion.106, bf16[96,128,128]{2,1,0:T(8,128)(2,1)S(1)} %copy-done.8), kind=kCustom, calls=%fused_computation.10 | custom fusion | bytes 9437568 | tf_op jit(solution)/shard_map/scatter | solution.py:64
  26.7 6.3 dynamic-slice_bitcast_fusion
  33.0 3.0 collective-permute-start
  37.5 2.6 collective-permute-start.2
  41.2 2.7 collective-permute-start.4
  45.6 3.3 all-to-all-start
  49.2 6.1 psum.119
  55.5 102.6 %all-to-all-done = s32[8,24,2]{1,2,0:T(2,128)S(1)} async-done(((s32[8,24,2]{1,2,0:T(2,128)}), s32[8,24,2]{1,2,0:T(2,128)S(1)}, u32[]{:S(2)}, u32[]{:S(2)}) %all-to-all-start) | async-done | bytes 1568 | tf_op jit(solution)/shard_map/all_to_all | solution.py:84
  158.2 2.7 gather_fusion.1
  162.4 2.1 bitcast_dynamic-update-slice_fusion.6
  165.6 2.1 bitcast_dynamic-update-slice_fusion.5
  167.8 2.2 bitcast_dynamic-update-slice_fusion.4
  169.9 2.1 bitcast_dynamic-update-slice_fusion.3
  172.0 2.1 bitcast_dynamic-update-slice_fusion.2
  174.2 7.3 collective-permute-done.5
  182.4 12.5 %collective-permute-done.6 = bf16[1,24,128,128]{3,2,1,0:T(8,128)(2,1)S(1)} collective-permute-done((bf16[1,24,128,128]{3,2,1,0:T(8,128)(2,1)S(1)}, bf16[1,24,128,128]{3,2,1,0:T(8,128)(2,1)S(1)}, u32[]{:S(2)}, u32[]{:S(2)}) %collective-permute-start.6) | collective-permute-done | bytes 786464 | tf_op jit(solution)/shard_map/ppermute | solution.py:78
  195.9 6.9 gather_fusion
  202.8 3.9 fusion.48
  206.8 5.8 fusion.14
  214.2 38.0 %all-reduce.9.cloned.1.call-done = f32[64,4096]{1,0:T(8,128)} async-done(((f32[64,4096]{1,0:T(8,128)}), f32[64,4096]{1,0:T(8,128)}) %all-reduce.9.cloned.1.call-update) | async-done | bytes 1048592 | tf_op jit(solution)/shard_map/psum | solution.py:97
  253.7 21.5 %psum.121 = f32[64]{0:T(128)S(1)} all-reduce(f32[64]{0:T(128)S(1)} %multiply_reduce_fusion.7), channel_id=1, replica_groups=mesh['row'=4,'col'=8] {'col'}, use_global_device_ids=true, to_apply=%region_8.10 | all-reduce | flops 64 | bytes 512 | tf_op jit(solution)/shard_map/psum | solution.py:111
  276.8 2.8 gather_fusion.2
  279.6 8.1 fusion.51
  287.7 5.8 fusion.12
  295.2 75.0 %all-reduce.11.cloned.1.call-done = f32[64,4096]{1,0:T(8,128)} async-done(((f32[64,4096]{1,0:T(8,128)}), f32[64,4096]{1,0:T(8,128)}) %all-reduce.11.cloned.1.call-update) | async-done | bytes 1048592 | tf_op jit(solution)/shard_map/psum | solution.py:126
  371.8 6.1 psum.123
  378.1 2.8 gather_fusion.3
  380.9 5.6 fusion.54
  386.4 5.7 fusion.10
  392.2 1.7 copy.117
  393.9 35.8 %all-reduce.13.cloned.1.call-done = f32[64,4096]{1,0:T(8,128)} async-done(((f32[64,4096]{1,0:T(8,128)}), f32[64,4096]{1,0:T(8,128)}) %all-reduce.13.cloned.1.call-update) | async-done | bytes 1048592 | tf_op jit(solution)/shard_map/psum | solution.py:97
  431.3 21.8 %psum.125 = f32[64]{0:T(128)S(1)} all-reduce(f32[64]{0:T(128)S(1)} %multiply_reduce_fusion.5), channel_id=1, replica_groups=mesh['row'=4,'col'=8] {'col'}, use_global_device_ids=true, to_apply=%region_14.16 | all-reduce | flops 64 | bytes 512 | tf_op jit(solution)/shard_map/psum | solution.py:111
  454.7 2.8 gather_fusion.4
  457.5 8.1 fusion.57
  465.6 5.8 fusion.8
  473.1 74.9 %all-reduce.15.cloned.1.call-done = f32[64,4096]{1,0:T(8,128)} async-done(((f32[64,4096]{1,0:T(8,128)}), f32[64,4096]{1,0:T(8,128)}) %all-reduce.15.cloned.1.call-update) | async-done | bytes 1048592 | tf_op jit(solution)/shard_map/psum | solution.py:126
  547.9 2.6 multiply_reduce_fusion.4
  550.5 6.1 psum.127
  558.0 2.8 gather_fusion.5
  560.8 5.6 fusion.60
  566.4 5.8 fusion.6
  573.8 35.8 %all-reduce.17.cloned.1.call-done = f32[64,4096]{1,0:T(8,128)} async-done(((f32[64,4096]{1,0:T(8,128)}), f32[64,4096]{1,0:T(8,128)}) %all-reduce.17.cloned.1.call-update) | async-done | bytes 1048592 | tf_op jit(solution)/shard_map/psum | solution.py:97
  611.2 21.6 %psum.129 = f32[64]{0:T(128)S(1)} all-reduce(f32[64]{0:T(128)S(1)} %multiply_reduce_fusion.3), channel_id=1, replica_groups=mesh['row'=4,'col'=8] {'col'}, use_global_device_ids=true, to_apply=%region_20.22 | all-reduce | flops 64 | bytes 512 | tf_op jit(solution)/shard_map/psum | solution.py:111
  632.8 2.5 convert_bitcast_fusion.2
  635.4 2.8 gather_fusion.6
  638.2 8.1 fusion.63
  646.3 5.8 fusion.4
  653.8 75.0 %all-reduce.19.cloned.1.call-done = f32[64,4096]{1,0:T(8,128)} async-done(((f32[64,4096]{1,0:T(8,128)}), f32[64,4096]{1,0:T(8,128)}) %all-reduce.19.cloned.1.call-update) | async-done | bytes 1048592 | tf_op jit(solution)/shard_map/psum | solution.py:126
  728.8 2.6 multiply_reduce_fusion.2
  731.3 6.3 psum.131
  739.1 2.8 gather_fusion.7
  741.9 5.6 fusion.66
  747.5 5.8 fusion.2
  753.3 1.7 copy.113
  755.0 35.8 %all-reduce.21.cloned.1.call-done = f32[64,4096]{1,0:T(8,128)} async-done(((f32[64,4096]{1,0:T(8,128)}), f32[64,4096]{1,0:T(8,128)}) %all-reduce.21.cloned.1.call-update) | async-done | bytes 1048592 | tf_op jit(solution)/shard_map/psum | solution.py:97
  792.4 21.5 %psum.133 = f32[64]{0:T(128)S(1)} all-reduce(f32[64]{0:T(128)S(1)} %multiply_reduce_fusion.1), channel_id=1, replica_groups=mesh['row'=4,'col'=8] {'col'}, use_global_device_ids=true, to_apply=%region_26.28 | all-reduce | flops 64 | bytes 512 | tf_op jit(solution)/shard_map/psum | solution.py:111
  813.9 2.6 convert_bitcast_fusion
  816.6 2.7 gather_fusion.8
  819.3 8.1 fusion.69
  827.4 5.8 fusion
  833.2 1.6 copy.112
  834.9 75.1 %all-reduce.23.cloned.1.call-done = f32[64,4096]{1,0:T(8,128)} async-done(((f32[64,4096]{1,0:T(8,128)}), f32[64,4096]{1,0:T(8,128)}) %all-reduce.23.cloned.1.call-update) | async-done | bytes 1048592 | tf_op jit(solution)/shard_map/psum | solution.py:126
  911.5 5.9 psum.135
  (103 shorter events, 39.1 us)
Async XLA Ops:
  7.2 6.8 copy-start.8
  26.7 17.2 %copy-start.9 = (s32[96]{0:T(128)S(1)}, s32[96]{0:T(128)}, u32[]{:S(2)}) copy-start(s32[96]{0:T(128)} %param.11) | copy-start | bytes 1156
  26.7 17.2 %copy-start.10 = (s32[96]{0:T(128)S(1)}, s32[96]{0:T(128)}, u32[]{:S(2)}) copy-start(s32[96]{0:T(128)} %param.10) | copy-start | bytes 1156
  26.7 22.2 %copy-start.2 = (f32[64,4096]{1,0:T(8,128)S(1)}, f32[64,4096]{1,0:T(8,128)}, u32[]{:S(2)}) copy-start(f32[64,4096]{1,0:T(8,128)} %param.7) | copy-start | bytes 3145732
  33.0 127.9 %collective-permute-start = (bf16[1,24,128,128]{3,2,1,0:T(8,128)(2,1)}, bf16[1,24,128,128]{3,2,1,0:T(8,128)(2,1)}, u32[]{:S(2)}, u32[]{:S(2)}) collective-permute-start(bf16[1,24,128,128]{3,2,1,0:T(8,128)(2,1)} %get-tuple-element.34), channel_id=1, source_target_pairs={{0,1},{1,2},{2,3},{3,4},{4,5},{5,6},{6,7},{7,0},{8,9},{9,10},{10,1... | collective-permute-start | bytes 2359304 | tf_op jit(solution)/shard_map/ppermute | solution.py:78
  36.0 128.5 %collective-permute-start.1 = (bf16[1,24,128,128]{3,2,1,0:T(8,128)(2,1)}, bf16[1,24,128,128]{3,2,1,0:T(8,128)(2,1)}, u32[]{:S(2)}, u32[]{:S(2)}) collective-permute-start(bf16[1,24,128,128]{3,2,1,0:T(8,128)(2,1)} %get-tuple-element.33), channel_id=1, source_target_pairs={{0,2},{1,3},{2,4},{3,5},{4,6},{5,7},{6,0},{7,1},{8,10},{9,11},{10,... | collective-permute-start | bytes 2359304 | tf_op jit(solution)/shard_map/ppermute | solution.py:78
  37.5 130.2 %collective-permute-start.2 = (bf16[1,24,128,128]{3,2,1,0:T(8,128)(2,1)}, bf16[1,24,128,128]{3,2,1,0:T(8,128)(2,1)}, u32[]{:S(2)}, u32[]{:S(2)}) collective-permute-start(bf16[1,24,128,128]{3,2,1,0:T(8,128)(2,1)} %get-tuple-element.32), channel_id=1, source_target_pairs={{0,3},{1,4},{2,5},{3,6},{4,7},{5,0},{6,1},{7,2},{8,11},{9,12},{10,... | collective-permute-start | bytes 2359304 | tf_op jit(solution)/shard_map/ppermute | solution.py:78
  40.1 129.9 %collective-permute-start.3 = (bf16[1,24,128,128]{3,2,1,0:T(8,128)(2,1)}, bf16[1,24,128,128]{3,2,1,0:T(8,128)(2,1)}, u32[]{:S(2)}, u32[]{:S(2)}) collective-permute-start(bf16[1,24,128,128]{3,2,1,0:T(8,128)(2,1)} %get-tuple-element.31), channel_id=1, source_target_pairs={{0,4},{1,5},{2,6},{3,7},{4,0},{5,1},{6,2},{7,3},{8,12},{9,13},{10,... | collective-permute-start | bytes 2359304 | tf_op jit(solution)/shard_map/ppermute | solution.py:78
  41.2 130.8 %collective-permute-start.4 = (bf16[1,24,128,128]{3,2,1,0:T(8,128)(2,1)}, bf16[1,24,128,128]{3,2,1,0:T(8,128)(2,1)}, u32[]{:S(2)}, u32[]{:S(2)}) collective-permute-start(bf16[1,24,128,128]{3,2,1,0:T(8,128)(2,1)} %get-tuple-element.30), channel_id=1, source_target_pairs={{0,5},{1,6},{2,7},{3,0},{4,1},{5,2},{6,3},{7,4},{8,13},{9,14},{10,... | collective-permute-start | bytes 2359304 | tf_op jit(solution)/shard_map/ppermute | solution.py:78
  45.6 112.5 %all-to-all-start = ((s32[8,24,2]{1,2,0:T(2,128)}), s32[8,24,2]{1,2,0:T(2,128)S(1)}, u32[]{:S(2)}, u32[]{:S(2)}) async-start(s32[8,24,2]{1,2,0:T(2,128)} %copy.46), calls=%async_computation | async-start | bytes 16384 | tf_op jit(solution)/shard_map/all_to_all | solution.py:84
  48.9 203.4 %all-reduce.9.cloned.1.call-start = ((), (), s32[]{:S(2)}) async-start(), calls=%async_computation.1 | async-start | bytes 2097152 | tf_op jit(solution)/shard_map/psum | solution.py:97
  160.9 20.5 %collective-permute-start.5 = (bf16[1,24,128,128]{3,2,1,0:T(8,128)(2,1)S(1)}, bf16[1,24,128,128]{3,2,1,0:T(8,128)(2,1)S(1)}, u32[]{:S(2)}, u32[]{:S(2)}) collective-permute-start(bf16[1,24,128,128]{3,2,1,0:T(8,128)(2,1)S(1)} %get-tuple-element.29), channel_id=1, source_target_pairs={{0,6},{1,7},{2,0},{3,1},{4,2},{5,3},{6,4},{7,5},{8,14},{9,15},{10,... | collective-permute-start | bytes 2359304 | tf_op jit(solution)/shard_map/ppermute | solution.py:78
  164.5 30.4 %collective-permute-start.6 = (bf16[1,24,128,128]{3,2,1,0:T(8,128)(2,1)S(1)}, bf16[1,24,128,128]{3,2,1,0:T(8,128)(2,1)S(1)}, u32[]{:S(2)}, u32[]{:S(2)}) collective-permute-start(bf16[1,24,128,128]{3,2,1,0:T(8,128)(2,1)S(1)} %get-tuple-element.28), channel_id=1, source_target_pairs={{0,7},{1,0},{2,1},{3,2},{4,3},{5,4},{6,5},{7,6},{8,15},{9,8},{10,9... | collective-permute-start | bytes 2359304 | tf_op jit(solution)/shard_map/ppermute | solution.py:78
  195.9 7.0 copy-start
  214.2 156.0 %all-reduce.11.cloned.1.call-start = ((), (), s32[]{:S(2)}) async-start(), calls=%async_computation.2 | async-start | bytes 2097152 | tf_op jit(solution)/shard_map/psum | solution.py:126
  287.7 82.5 %copy-start.3 = (f32[64,4096]{1,0:T(8,128)S(1)}, f32[64,4096]{1,0:T(8,128)}, u32[]{:S(2)}) copy-start(f32[64,4096]{1,0:T(8,128)} %param.7) | copy-start | bytes 3145732
  295.1 134.7 %all-reduce.13.cloned.1.call-start = ((), (), s32[]{:S(2)}) async-start(), calls=%async_computation.3 | async-start | bytes 2097152 | tf_op jit(solution)/shard_map/psum | solution.py:97
  371.7 14.7 %copy-start.6 = (f32[64,4096]{1,0:T(8,128)}, f32[64,4096]{1,0:T(8,128)S(1)}, u32[]{:S(2)}) copy-start(f32[64,4096]{1,0:T(8,128)S(1)} %get-tuple-element.25) | copy-start | bytes 3145732
  393.9 154.0 %all-reduce.15.cloned.1.call-start = ((), (), s32[]{:S(2)}) async-start(), calls=%async_computation.4 | async-start | bytes 2097152 | tf_op jit(solution)/shard_map/psum | solution.py:126
  465.6 82.4 %copy-start.7 = (f32[64,4096]{1,0:T(8,128)S(1)}, f32[64,4096]{1,0:T(8,128)}, u32[]{:S(2)}) copy-start(f32[64,4096]{1,0:T(8,128)} %copy-done.6) | copy-start | bytes 3145732
  473.0 136.7 %all-reduce.17.cloned.1.call-start = ((), (), s32[]{:S(2)}) async-start(), calls=%async_computation.5 | async-start | bytes 2097152 | tf_op jit(solution)/shard_map/psum | solution.py:97
  573.8 155.0 %all-reduce.19.cloned.1.call-start = ((), (), s32[]{:S(2)}) async-start(), calls=%async_computation.6 | async-start | bytes 2097152 | tf_op jit(solution)/shard_map/psum | solution.py:126
  646.3 82.5 %copy-start.5 = (f32[64,4096]{1,0:T(8,128)S(1)}, f32[64,4096]{1,0:T(8,128)}, u32[]{:S(2)}) copy-start(f32[64,4096]{1,0:T(8,128)} %get-tuple-element.21) | copy-start | bytes 3145732
  653.8 137.1 %all-reduce.21.cloned.1.call-start = ((), (), s32[]{:S(2)}) async-start(), calls=%async_computation.7 | async-start | bytes 2097152 | tf_op jit(solution)/shard_map/psum | solution.py:97
  747.5 43.4 %copy-start.1 = (f32[64,4096]{1,0:T(8,128)S(1)}, f32[64,4096]{1,0:T(8,128)}, u32[]{:S(2)}) copy-start(f32[64,4096]{1,0:T(8,128)} %get-tuple-element.19) | copy-start | bytes 3145732
  755.0 155.0 %all-reduce.23.cloned.1.call-start = ((), (), s32[]{:S(2)}) async-start(), calls=%async_computation.8 | async-start | bytes 2097152 | tf_op jit(solution)/shard_map/psum | solution.py:126
  827.4 82.6 %copy-start.4 = (f32[64,4096]{1,0:T(8,128)S(1)}, f32[64,4096]{1,0:T(8,128)}, u32[]{:S(2)}) copy-start(f32[64,4096]{1,0:T(8,128)} %get-tuple-element.17) | copy-start | bytes 3145732
Sparse Core Ops, SparseCore 0:
  214.3 37.9 all-reduce.8
  295.2 74.8 all-reduce.10
  394.0 35.7 all-reduce.12
  473.1 74.7 all-reduce.14
  573.9 35.7 all-reduce.16
  653.9 74.8 all-reduce.18
  755.1 35.7 all-reduce.20
  835.0 74.9 all-reduce.22
